TPU v7x, 256 devices: a whole 4x4x8 slice. The times are simulated.
256 devices in a mesh: ctx: 16 (over z, core), tp: 16 (over x, y).
Axes of the slice: x: 4, y: 4, z: 8, core: 2. Of those that a mesh axis runs over, the one named last changes fastest.
Arguments:
- q_act: bfloat16 [64, 128, 4096], P('ctx', None, 'tp'), may hold values from -16 to 16
- k_act: bfloat16 [64, 128, 4096], P('ctx', None, 'tp'), may hold values from -16 to 16
- v_act: bfloat16 [64, 128, 4096], P('ctx', None, 'tp'), may hold values from -6 to 6
- grad_out: bfloat16 [8192, 4096], P(('ctx', 'tp')), may hold values from -24 to 24
- w_out: bfloat16 [4096, 4096], P(None, 'tp'), may hold values from -0.09375 to 0.09375
- nbr_tiles: int32 [64, 12], replicated, may hold values from 0 to 63, as said below
- nbr_valid: int32 [64, 12], replicated, may hold values from 0 to 1, as said below
- slot_of: int32 [64], replicated, may hold values from 0 to 63, as said below
Outputs:
- grad_q: bfloat16 [64, 128, 4096], P('ctx', None, 'tp')
- grad_k: bfloat16 [64, 128, 4096], P('ctx', None, 'tp')
- grad_v: bfloat16 [64, 128, 4096], P('ctx', None, 'tp')
- grad_w_out: bfloat16 [4096, 4096], P('ctx', 'tp')
Inputs may be any that keep to these rules, and one draw needn't show every extreme that they name: `nbr_tiles`: row t lists scenario tiles linked to tile t; the live entries of a row name distinct tiles, one of them t itself. `nbr_valid`: every row has at least one live entry; a tile is named by live entries of at most 12 rows. `slot_of`: a permutation; slots c * 4 to c * 4 + 3 are held by index c of ctx.
All inputs are finite; a program needn't handle non-finite values.
Results may differ from a plain program's by a relative error of at most 0.024.
Values may be sent and summed in bfloat16 or wider, within the bound.
No kernel may reach another device: no remote copies, remote signals or barrier semaphores. Data moves between devices by JAX's collectives and lax.ppermute only.
A program may use at most 128 MiB of HBM per device.

v0:
```python
import math

import jax
import jax.numpy as jnp
from jax import lax
from jax.sharding import PartitionSpec as P

HD = 128


def side_by_side(arrays, axis, dim, along):
    widths = [a.shape[along] for a in arrays]
    both = jnp.concatenate(arrays, axis=along)
    out = lax.all_gather(both, axis, axis=dim, tiled=True)
    return tuple(jnp.split(out, [sum(widths[:k]) for k in range(1, len(widths))], axis=along))


def slot_tables(nbr_tiles, nbr_valid, slot_of):
    tile_count = slot_of.shape[0]
    slot_index = jnp.arange(tile_count, dtype=jnp.int32)
    matches = (slot_of[:, None] == slot_index[None, :]).astype(jnp.int32)
    near_tiles = jnp.einsum("ts,tj->sj", matches, nbr_tiles)
    live_mask = jnp.einsum("ts,tj->sj", matches, nbr_valid)
    found = (near_tiles[:, :, None] == slot_index[None, None, :]).astype(jnp.int32)
    key_slot = jnp.sum(found * slot_of[None, None, :], axis=2)
    return (key_slot, live_mask)


def per_device(q_act, k_act, v_act, grad_out, w_out, nbr_tiles, nbr_valid, slot_of):
    local_tiles, tile_len, col_width = q_act.shape
    head_count = col_width // HD
    score_scale = 1.0 / math.sqrt(HD)
    ctx_count = lax.axis_size("ctx")
    tile_count = local_tiles * ctx_count
    first_slot = lax.axis_index("ctx") * local_tiles
    key_slot, live_mask = slot_tables(nbr_tiles, nbr_valid, slot_of)
    near_slots = lax.dynamic_slice_in_dim(key_slot, first_slot, local_tiles, 0)
    near_live = lax.dynamic_slice_in_dim(live_mask, first_slot, local_tiles, 0)
    list_len = near_slots.shape[1]
    full_rows = lax.all_gather(grad_out, "tp", axis=0, tiled=True)
    grad_flat = jnp.dot(full_rows, w_out, preferred_element_type=jnp.float32).astype(jnp.bfloat16)
    grad_tiles = grad_flat.reshape(local_tiles, tile_len, col_width)
    grad_grid = grad_flat.reshape(local_tiles, tile_len, head_count, HD)
    key_all, value_all = side_by_side((k_act, v_act), "ctx", 0, 1)
    near_keys = key_all[near_slots].reshape(local_tiles, list_len, tile_len, head_count, HD)
    near_values = value_all[near_slots].reshape(local_tiles, list_len, tile_len, head_count, HD)
    query_grid = q_act.reshape(local_tiles, tile_len, head_count, HD)
    live_cells = (near_live > 0)[:, None, None, :, None]
    scores = (
        jnp.einsum("sahd,sjbhd->shajb", query_grid, near_keys, preferred_element_type=jnp.float32)
        * score_scale
    )
    row_peak = jnp.max(jnp.where(live_cells, scores, -1e30), axis=(3, 4), keepdims=True)
    row_total = jnp.sum(
        jnp.where(live_cells, jnp.exp(scores - row_peak), 0.0), axis=(3, 4), keepdims=True
    )
    log_total = row_peak + jnp.log(row_total)
    prob_full = jnp.where(live_cells, jnp.exp(scores - log_total), 0.0)
    prob_half = prob_full.astype(jnp.bfloat16)
    attn_grid = jnp.einsum(
        "shajb,sjbhd->sahd", prob_half, near_values, preferred_element_type=jnp.float32
    ).astype(jnp.bfloat16)
    row_delta = jnp.einsum(
        "sahd,sahd->sha", grad_grid, attn_grid, preferred_element_type=jnp.float32
    )
    grad_prob = jnp.einsum(
        "sahd,sjbhd->shajb", grad_grid, near_values, preferred_element_type=jnp.float32
    )
    grad_score = (prob_full * (grad_prob - row_delta[:, :, :, None, None])).astype(jnp.bfloat16)
    grad_query = (
        jnp.einsum("shajb,sjbhd->sahd", grad_score, near_keys, preferred_element_type=jnp.float32)
        * score_scale
    )
    grad_q = grad_query.astype(jnp.bfloat16).reshape(local_tiles, tile_len, col_width)
    query_all, grad_all = (
        lax.all_gather(q_act, "ctx", axis=0, tiled=True),
        lax.all_gather(grad_tiles, "ctx", axis=0, tiled=True),
    )
    total_all, delta_all = side_by_side((log_total[:, :, :, 0, 0], row_delta), "ctx", 0, 1)
    query_wide = query_all.reshape(tile_count, tile_len, head_count, HD)
    grad_wide = grad_all.reshape(tile_count, tile_len, head_count, HD)
    owned_slots = first_slot + jnp.arange(local_tiles, dtype=jnp.int32)
    pair_hits = (key_slot[:, :, None] == owned_slots[None, None, :]) & (live_mask[:, :, None] > 0)
    named_by = jnp.any(pair_hits, axis=1).astype(jnp.int32)
    rank_of = jnp.cumsum(named_by, axis=0) - 1
    list_pos = jnp.arange(list_len, dtype=jnp.int32)
    placed = (named_by[:, :, None] > 0) & (rank_of[:, :, None] == list_pos[None, None, :])
    slot_index = jnp.arange(tile_count, dtype=jnp.int32)
    picked = jnp.sum(placed.astype(jnp.int32) * slot_index[:, None, None], axis=0)
    picked_live = jnp.any(placed, axis=0)

    def owner_grads(inputs):
        key_tile, value_tile, chosen, chosen_live = inputs
        query_rows = query_wide[chosen]
        grad_rows = grad_wide[chosen]
        total_rows = total_all[chosen]
        delta_rows = delta_all[chosen]
        owner_scores = (
            jnp.einsum("tahd,bhd->thab", query_rows, key_tile, preferred_element_type=jnp.float32)
            * score_scale
        )
        keep_pair = chosen_live[:, None, None, None]
        owner_probs = jnp.where(keep_pair, jnp.exp(owner_scores - total_rows[:, :, :, None]), 0.0)
        owner_grad_prob = jnp.einsum(
            "tahd,bhd->thab", grad_rows, value_tile, preferred_element_type=jnp.float32
        )
        owner_grad_score = (owner_probs * (owner_grad_prob - delta_rows[:, :, :, None])).astype(
            jnp.bfloat16
        )
        grad_key = (
            jnp.einsum(
                "thab,tahd->bhd", owner_grad_score, query_rows, preferred_element_type=jnp.float32
            )
            * score_scale
        )
        grad_value = jnp.einsum(
            "thab,tahd->bhd",
            owner_probs.astype(jnp.bfloat16),
            grad_rows,
            preferred_element_type=jnp.float32,
        )
        return (grad_key.astype(jnp.bfloat16), grad_value.astype(jnp.bfloat16))

    key_local = k_act.reshape(local_tiles, tile_len, head_count, HD)
    value_local = v_act.reshape(local_tiles, tile_len, head_count, HD)
    grad_key_all, grad_value_all = lax.map(
        owner_grads, (key_local, value_local, picked, picked_live)
    )
    grad_k = grad_key_all.reshape(local_tiles, tile_len, col_width)
    grad_v = grad_value_all.reshape(local_tiles, tile_len, col_width)
    attn_flat = attn_grid.reshape(local_tiles * tile_len, col_width)
    grad_weight = lax.psum_scatter(
        lax.dot_general(
            full_rows, attn_flat, (((0,), (0,)), ((), ())), preferred_element_type=jnp.float32
        ).astype(jnp.bfloat16),
        "ctx",
        scatter_dimension=0,
        tiled=True,
    )
    return (grad_q, grad_k, grad_v, grad_weight)


def solution(mesh):
    in_specs = (
        P("ctx", None, "tp"),
        P("ctx", None, "tp"),
        P("ctx", None, "tp"),
        P(("ctx", "tp"), None),
        P(None, "tp"),
        P(),
        P(),
        P(),
    )
    out_specs = (P("ctx", None, "tp"), P("ctx", None, "tp"), P("ctx", None, "tp"), P("ctx", "tp"))
    return jax.shard_map(
        per_device, mesh=mesh, in_specs=in_specs, out_specs=out_specs, check_vma=False
    )
```

profile of v0, /device:TPU:1, one launch (start us, length us, event | category | flops | bytes accessed | tf_op | source)
XLA Modules:
  0.0 342.1 jit_solution(13095757694921598269)
XLA Ops:
  8.7 1.9 pad_maximum_fusion
  10.8 59.7 %all-gather.7.cloned.1.call-done = bf16[512,4096]{1,0:T(8,128)(2,1)} async-done(((bf16[32,4096]{1,0:T(8,128)(2,1)}), bf16[512,4096]{1,0:T(8,128)(2,1)}) %all-gather.7.cloned.1.call-update) | async-done | bytes 4194320 | tf_op jit(solution)/shard_map/all_gather | solution.py:40
  70.5 4.1 %convolution_convert_fusion.1 = bf16[512,256]{1,0:T(8,128)(2,1)} fusion(bf16[512,4096]{1,0:T(8,128)(2,1)} %all-gather.7.cloned.1.call-done, bf16[4096,256]{1,0:T(8,128)(2,1)S(1)} %copy-done), kind=kOutput, calls=%fused_computation.56 | convolution fusion | flops 1073872896 | bytes 6553600 | tf_op jit(solution)/shard_map/dot_general | solution.py:41
  81.3 33.3 %all-gather.9.cloned.1.call-done = bf16[64,128,256]{2,1,0:T(8,128)(2,1)} async-done(((bf16[4,128,256]{2,1,0:T(8,128)(2,1)}), bf16[64,128,256]{2,1,0:T(8,128)(2,1)}) %all-gather.9.cloned.1.call-update) | async-done | bytes 4194320 | tf_op jit(solution)/shard_map/all_gather | solution.py:76
  114.5 6.9 %reshape.119 = bf16[64,128,2,128]{3,2,1,0:T(2,128)(2,1)} reshape(bf16[64,128,256]{2,1,0:T(8,128)(2,1)} %all-gather.9.cloned.1.call-done) | data formatting | bytes 8388608 | tf_op jit(solution)/shard_map/reshape | solution.py:80
  121.5 49.4 %all-gather.5.cloned.1.call-done = bf16[64,256,256]{2,1,0:T(8,128)(2,1)} async-done(((bf16[4,256,256]{2,1,0:T(8,128)(2,1)}), bf16[64,256,256]{2,1,0:T(8,128)(2,1)}) %all-gather.5.cloned.1.call-update) | async-done | bytes 8388624 | tf_op jit(solution)/shard_map/all_gather | solution.py:14
  170.8 6.0 %fusion.65 = (bf16[64,128,256]{2,1,0:T(8,128)(2,1)}, bf16[64,128,256]{2,1,0:T(8,128)(2,1)}) fusion(bf16[64,256,256]{2,1,0:T(8,128)(2,1)} %all-gather.5.cloned.1.call-done), kind=kLoop, calls=%fused_computation.91 | loop fusion | bytes 16777216 | tf_op jit(solution)/shard_map/split | solution.py:15
  176.9 2.9 gather_fusion.4
  179.8 3.0 reshape.114
  182.8 7.2 %copy.136 = bf16[4,12,128,2,128]{2,4,1,3,0:T(8,128)(2,1)S(1)} copy(bf16[4,12,128,2,128]{4,3,2,1,0:T(2,128)(2,1)} %reshape.114) | data formatting | bytes 6291456 | tf_op jit(solution)/shard_map/reshape | solution.py:45
  190.1 4.7 %gather_fusion.5 = bf16[48,128,256]{2,1,0:T(8,128)(2,1)} fusion(bf16[64,128,256]{2,1,0:T(8,128)(2,1)} %get-tuple-element.150, s32[1024]{0:T(1024)S(1)} %pad_clamp_fusion.1), kind=kCustom, calls=%fused_computation.5 | custom fusion | bytes 6291648 | tf_op jit(solution)/shard_map/gather | solution.py:46
  194.8 5.5 %reshape.117 = bf16[4,12,128,2,128]{4,3,2,1,0:T(2,128)(2,1)} reshape(bf16[48,128,256]{2,1,0:T(8,128)(2,1)} %gather_fusion.5) | data formatting | bytes 6291456 | tf_op jit(solution)/shard_map/reshape | solution.py:46
  200.3 8.6 %copy.133 = bf16[4,12,128,2,128]{2,4,1,3,0:T(8,128)(2,1)} copy(bf16[4,12,128,2,128]{4,3,2,1,0:T(2,128)(2,1)} %reshape.117) | data formatting | bytes 6291456 | tf_op jit(solution)/shard_map/reshape | solution.py:46
  209.0 1.9 select_reduce_fusion.1
  215.1 2.4 multiply_reduce_fusion
  217.6 7.6 %fusion.45 = bf16[4,2,128,128]{3,2,1,0:T(8,128)(2,1)} fusion(bf16[4,12,128,2,128]{2,4,1,3,0:T(8,128)(2,1)S(1)} %copy.136, f32[4,2,12,128,128]{4,3,2,1,0:T(8,128)} %copy-done.2, f32[4,2,128]{2,1,0:T(2,128)S(1)} %get-tuple-element.160, f32[4,2,128]{2,1,0:T(2,128)S(1)} %bitcast.194, pred[4,12]{1,0:T(4,128)(4,1)S(1)} %copy.128, ...), kind=kOutput, calls=%fused_computation.55 | convolution fusion | flops 815005696 | bytes 13115440 | tf_op jit(solution)/shard_map/shajb,sjbhd->sahd/dot_general | solution.py:71
  228.0 16.2 %all_gather.18 = f32[64,4,128]{2,1,0:T(4,128)S(1)} all-gather(f32[4,4,128]{2,1,0:T(4,128)S(1)} %pad_maximum_fusion.1), channel_id=1, replica_groups=mesh['ctx'=16,'tp'=16] {'ctx'}, dimensions={0}, use_global_device_ids=true | all-gather | bytes 139264 | tf_op jit(solution)/shard_map/all_gather | solution.py:14
  244.9 4.8 %fusion.27 = bf16[4096,256]{0,1:T(8,128)(2,1)} fusion(bf16[512,4096]{1,0:T(8,128)(2,1)} %all-gather.7.cloned.1.call-done, bf16[64,8,2,128]{3,2,1,0:T(2,128)(2,1)S(1)} %bitcast.185), kind=kOutput, calls=%fused_computation.43 | convolution fusion | flops 1074790400 | bytes 6553600 | tf_op jit(solution)/shard_map/dot_general | solution.py:133
  249.8 7.0 %reshape.123 = bf16[64,128,2,128]{3,2,1,0:T(2,128)(2,1)} reshape(bf16[64,128,256]{2,1,0:T(8,128)(2,1)} %all-gather.11.cloned.1.call-done) | data formatting | bytes 8388608 | tf_op jit(solution)/shard_map/reshape | solution.py:81
  256.7 74.5 %while.12 = (s32[]{:T(128)}, bf16[4,128,2,128]{1,3,2,0:T(8,128)(2,1)S(1)}, bf16[4,128,2,128]{1,3,2,0:T(8,128)(2,1)}, s32[4,12]{1,0:T(4,128)S(1)}, bf16[64,128,2,...) while((s32[]{:T(128)}, ...), condition=%wide.region_8.9_spmd, body=%wide.region_7.8_spmd.sunk | while | flops 405505056 | bytes 14550529 | solution.py:126
  256.8 4.3 %gather_fusion = bf16[12,128,2,128]{3,2,1,0:T(2,128)(2,1)S(1)} fusion(bf16[64,128,2,128]{3,2,1,0:T(2,128)(2,1)} %get-tuple-element.257, s32[1024]{0:T(1024)S(1)} %pad_clamp_fusion.3), kind=kCustom, calls=%fused_computation.clone.1 | custom fusion | bytes 1572912 | tf_op jit(solution)/shard_map/while/body/eval_jaxpr/gather | solution.py:94
  264.6 5.3 %gather_fusion.2 = bf16[12,128,2,128]{3,2,1,0:T(2,128)(2,1)} fusion(bf16[64,128,2,128]{3,2,1,0:T(2,128)(2,1)} %get-tuple-element.262, s32[1024]{0:T(1024)S(1)} %pad_clamp_fusion.3), kind=kCustom, calls=%fused_computation.2.clone.1 | custom fusion | bytes 1572912 | tf_op jit(solution)/shard_map/while/body/eval_jaxpr/gather | solution.py:95
  269.9 2.3 copy.196
  275.4 4.3 %gather_fusion = bf16[12,128,2,128]{3,2,1,0:T(2,128)(2,1)S(1)} fusion(bf16[64,128,2,128]{3,2,1,0:T(2,128)(2,1)} %get-tuple-element.257, s32[1024]{0:T(1024)S(1)} %pad_clamp_fusion.3), kind=kCustom, calls=%fused_computation.clone.1 | custom fusion | bytes 1572912 | tf_op jit(solution)/shard_map/while/body/eval_jaxpr/gather | solution.py:94
  283.2 5.3 %gather_fusion.2 = bf16[12,128,2,128]{3,2,1,0:T(2,128)(2,1)} fusion(bf16[64,128,2,128]{3,2,1,0:T(2,128)(2,1)} %get-tuple-element.262, s32[1024]{0:T(1024)S(1)} %pad_clamp_fusion.3), kind=kCustom, calls=%fused_computation.2.clone.1 | custom fusion | bytes 1572912 | tf_op jit(solution)/shard_map/while/body/eval_jaxpr/gather | solution.py:95
  288.6 2.3 copy.196
  294.0 4.3 %gather_fusion = bf16[12,128,2,128]{3,2,1,0:T(2,128)(2,1)S(1)} fusion(bf16[64,128,2,128]{3,2,1,0:T(2,128)(2,1)} %get-tuple-element.257, s32[1024]{0:T(1024)S(1)} %pad_clamp_fusion.3), kind=kCustom, calls=%fused_computation.clone.1 | custom fusion | bytes 1572912 | tf_op jit(solution)/shard_map/while/body/eval_jaxpr/gather | solution.py:94
  301.8 5.3 %gather_fusion.2 = bf16[12,128,2,128]{3,2,1,0:T(2,128)(2,1)} fusion(bf16[64,128,2,128]{3,2,1,0:T(2,128)(2,1)} %get-tuple-element.262, s32[1024]{0:T(1024)S(1)} %pad_clamp_fusion.3), kind=kCustom, calls=%fused_computation.2.clone.1 | custom fusion | bytes 1572912 | tf_op jit(solution)/shard_map/while/body/eval_jaxpr/gather | solution.py:95
  307.2 2.3 copy.196
  312.6 4.3 %gather_fusion = bf16[12,128,2,128]{3,2,1,0:T(2,128)(2,1)S(1)} fusion(bf16[64,128,2,128]{3,2,1,0:T(2,128)(2,1)} %get-tuple-element.257, s32[1024]{0:T(1024)S(1)} %pad_clamp_fusion.3), kind=kCustom, calls=%fused_computation.clone.1 | custom fusion | bytes 1572912 | tf_op jit(solution)/shard_map/while/body/eval_jaxpr/gather | solution.py:94
  320.5 5.3 %gather_fusion.2 = bf16[12,128,2,128]{3,2,1,0:T(2,128)(2,1)} fusion(bf16[64,128,2,128]{3,2,1,0:T(2,128)(2,1)} %get-tuple-element.262, s32[1024]{0:T(1024)S(1)} %pad_clamp_fusion.3), kind=kCustom, calls=%fused_computation.2.clone.1 | custom fusion | bytes 1572912 | tf_op jit(solution)/shard_map/while/body/eval_jaxpr/gather | solution.py:95
  325.8 2.3 copy.196
  (121 shorter events, 46.7 us)
Async XLA Ops:
  7.2 63.3 %copy-start = (bf16[4096,256]{1,0:T(8,128)(2,1)S(1)}, bf16[4096,256]{1,0:T(8,128)(2,1)}, u32[]{:S(2)}) copy-start(bf16[4096,256]{1,0:T(8,128)(2,1)} %param.14) | copy-start | bytes 6291460
  7.2 63.3 %all-gather.7.cloned.1.call-start = ((), (), s32[]{:S(2)}) async-start(), calls=%async_computation.2 | async-start | bytes 4456448 | tf_op jit(solution)/shard_map/all_gather | solution.py:40
  7.9 106.6 %all-gather.9.cloned.1.call-start = ((), (), s32[]{:S(2)}) async-start(), calls=%async_computation.3 | async-start | bytes 4456448 | tf_op jit(solution)/shard_map/all_gather | solution.py:76
  8.7 162.2 %all-gather.5.cloned.1.call-start = ((), (), s32[]{:S(2)}) async-start(), calls=%async_computation.1 | async-start | bytes 8912896 | tf_op jit(solution)/shard_map/all_gather | solution.py:14
  10.6 64.1 %copy-start.6 = (bf16[4,128,256]{2,1,0:T(8,128)(2,1)S(1)}, bf16[4,128,256]{2,1,0:T(8,128)(2,1)}, u32[]{:S(2)}) copy-start(bf16[4,128,256]{2,1,0:T(8,128)(2,1)} %param.10) | copy-start | bytes 786436
  10.7 64.2 %copy-start.7 = (bf16[4,128,256]{2,1,0:T(8,128)(2,1)S(1)}, bf16[4,128,256]{2,1,0:T(8,128)(2,1)}, u32[]{:S(2)}) copy-start(bf16[4,128,256]{2,1,0:T(8,128)(2,1)} %param.11) | copy-start | bytes 786436
  10.7 65.0 %copy-start.8 = (bf16[4,128,256]{2,1,0:T(8,128)(2,1)S(1)}, bf16[4,128,256]{2,1,0:T(8,128)(2,1)}, u32[]{:S(2)}) copy-start(bf16[4,128,256]{2,1,0:T(8,128)(2,1)} %param.12) | copy-start | bytes 786436
  10.7 65.9 %copy-start.11 = (s32[64]{0:T(128)S(1)}, s32[64]{0:T(128)}, u32[]{:S(2)}) copy-start(s32[64]{0:T(128)} %param.17) | copy-start | bytes 772
  10.7 65.9 %copy-start.12 = (s32[64,12]{0,1:T(8,128)S(1)}, s32[64,12]{0,1:T(8,128)}, u32[]{:S(2)}) copy-start(s32[64,12]{0,1:T(8,128)} %param.15) | copy-start | bytes 9220
  10.7 66.7 %copy-start.13 = (s32[64,12]{0,1:T(8,128)S(1)}, s32[64,12]{0,1:T(8,128)}, u32[]{:S(2)}) copy-start(s32[64,12]{0,1:T(8,128)} %param.16) | copy-start | bytes 9220
  10.7 239.1 %all-gather.11.cloned.1.call-start = ((), (), s32[]{:S(2)}) async-start(), calls=%async_computation.4 | async-start | bytes 4456448 | tf_op jit(solution)/shard_map/all_gather | solution.py:77
  74.7 259.2 %reduce-scatter.2.cloned.1.call-start = ((), (), s32[]{:S(2)}) async-start(), calls=%async_computation.5 | async-start | bytes 2228224 | tf_op jit(solution)/shard_map/reduce_scatter | solution.py:132
  80.1 41.4 %copy-start.4 = (bf16[4,128,2,128]{3,2,1,0:T(2,128)(2,1)}, bf16[4,128,2,128]{3,2,1,0:T(2,128)(2,1)S(1)}, u32[]{:S(2)}) copy-start(bf16[4,128,2,128]{3,2,1,0:T(2,128)(2,1)S(1)} %reshape.116) | copy-start | bytes 786436
  210.9 3.2 copy-start.2
  210.9 4.2 %copy-start.3 = (bf16[4,12,128,2,128]{2,4,1,3,0:T(8,128)(2,1)S(1)}, bf16[4,12,128,2,128]{2,4,1,3,0:T(8,128)(2,1)}, u32[]{:S(2)}) copy-start(bf16[4,12,128,2,128]{2,4,1,3,0:T(8,128)(2,1)} %copy.133) | copy-start | bytes 9437188
  210.9 4.2 %copy-start.9 = (f32[4,2,128,128]{2,3,1,0:T(8,128)S(1)}, f32[4,2,128,128]{2,3,1,0:T(8,128)}, u32[]{:S(2)}) copy-start(f32[4,2,128,128]{2,3,1,0:T(8,128)} %copy.167) | copy-start | bytes 1572868
  215.1 2.4 copy-start.5
  249.7 7.0 %copy-start.10 = (bf16[4,128,2,128]{1,3,2,0:T(8,128)(2,1)S(1)}, bf16[4,128,2,128]{1,3,2,0:T(8,128)(2,1)}, u32[]{:S(2)}) copy-start(bf16[4,128,2,128]{1,3,2,0:T(8,128)(2,1)} %custom-call.12) | copy-start | bytes 786436
  331.2 4.3 %copy-start.1 = (bf16[4096,256]{1,0:T(8,128)(2,1)S(1)}, bf16[4096,256]{1,0:T(8,128)(2,1)}, u32[]{:S(2)}) copy-start(bf16[4096,256]{1,0:T(8,128)(2,1)} %param.14) | copy-start | bytes 6291460
Sparse Core Ops, SparseCore 0:
  10.4 60.0 all-gather.6
  72.3 42.1 all-gather.8
  116.4 54.3 all-gather.4
  173.1 40.4 all-gather.10
  249.9 56.4 reduce-scatter.1
where the time goes:
time: 344 us; the launch traced here: 342 us
  waiting for transfers between devices  144 us (42%)
  local copies, waits for them, and re-layouts  126 us (37%)
  matrix products  36.7 us (11%)
  blocking collectives  16.2 us (5%)
  between operations  14 us (4%)
  other arithmetic  4.96 us (1%)
    all_gather x1, waiting for transfers between devices, per_device(): full_rows = lax.all_gather(grad_out, 'tp', axis=0, tiled=True)  59.7 us
    all_gather x1, waiting for transfers between devices, side_by_side(): out = lax.all_gather(both, axis, axis=dim, tiled=True)  49.4 us
    all_gather x1, waiting for transfers between devices, per_device(): lax.all_gather(q_act, 'ctx', axis=0, tiled=True)  33.3 us
    gather x8, local copies, waits for them, and re-layouts, owner_grads(): grad_rows = grad_wide[chosen]  30.6 us
    gather x8, local copies, waits for them, and re-layouts, owner_grads(): query_rows = query_wide[chosen]  20.1 us
    all_gather x1, blocking collectives, side_by_side(): out = lax.all_gather(both, axis, axis=dim, tiled=True)  16.2 us
    reshape x2, local copies, waits for them, and re-layouts, per_device(): value_all[near_slots]  14.2 us
    reshape x2, local copies, waits for them, and re-layouts, per_device(): key_all[near_slots].reshape(local_tiles, list_len, tile_len, head_count, HD)  10.3 us
  transfers between devices with their start and end apart: 5, of which 3 were waited for; matrix products, arithmetic and copies ran while one was open for 48% of the time, Pallas kernels for 0%

commit v1 on v0

v1 whole, which is shorter than its diff:
```python
import math

import jax
import jax.numpy as jnp
from jax import lax
from jax.sharding import Mesh
from jax.sharding import PartitionSpec as P

HD = 128
CORES = 2


def slot_tables(nbr_tiles, nbr_valid, slot_of):
    tile_count = slot_of.shape[0]
    slot_index = jnp.arange(tile_count, dtype=jnp.int32)
    matches = (slot_of[:, None] == slot_index[None, :]).astype(jnp.int32)
    near_tiles = jnp.einsum("ts,tj->sj", matches, nbr_tiles)
    live_mask = jnp.einsum("ts,tj->sj", matches, nbr_valid)
    found = (near_tiles[:, :, None] == slot_index[None, None, :]).astype(jnp.int32)
    key_slot = jnp.sum(found * slot_of[None, None, :], axis=2)
    return (key_slot, live_mask)


def to_head(arrays, local_tiles, tile_len, heads_here):
    stacked = jnp.stack(
        [a.reshape(local_tiles, tile_len, heads_here, HD) for a in arrays], axis=1
    )
    moved = lax.all_to_all(stacked, "core", split_axis=3, concat_axis=0, tiled=True)
    return moved.reshape(local_tiles * heads_here, len(arrays), tile_len, HD)


def from_head(arrays, local_tiles, tile_len, heads_here):
    stacked = jnp.stack(arrays, axis=1)[:, :, :, None, :]
    moved = lax.all_to_all(stacked, "core", split_axis=0, concat_axis=3, tiled=True)
    return tuple(
        moved[:, n].reshape(local_tiles, tile_len, heads_here * HD) for n in range(len(arrays))
    )


def per_device(q_act, k_act, v_act, grad_out, w_out, nbr_tiles, nbr_valid, slot_of):
    local_tiles, tile_len, col_width = q_act.shape
    heads_here = col_width // HD
    score_scale = 1.0 / math.sqrt(HD)
    chip_tiles = local_tiles * heads_here
    first_slot = lax.axis_index("z") * chip_tiles
    key_slot, live_mask = slot_tables(nbr_tiles, nbr_valid, slot_of)
    tile_count = key_slot.shape[0]
    list_len = key_slot.shape[1]
    near_slots = lax.dynamic_slice_in_dim(key_slot, first_slot, chip_tiles, 0)
    near_live = lax.dynamic_slice_in_dim(live_mask, first_slot, chip_tiles, 0)

    full_rows = lax.all_gather(grad_out, "tp", axis=0, tiled=True)
    grad_flat = jnp.dot(full_rows, w_out, preferred_element_type=jnp.float32).astype(jnp.bfloat16)
    grad_tiles = grad_flat.reshape(local_tiles, tile_len, col_width)

    head_parts = to_head((q_act, k_act, v_act, grad_tiles), local_tiles, tile_len, heads_here)
    query_h = head_parts[:, 0]
    key_h = head_parts[:, 1]
    value_h = head_parts[:, 2]
    grad_h = head_parts[:, 3]

    kv_all = lax.all_gather(head_parts[:, 1:3], "z", axis=0, tiled=True)
    near = kv_all[near_slots.reshape(-1)].reshape(chip_tiles, list_len, 2, tile_len, HD)
    near_keys = near[:, :, 0].reshape(chip_tiles, list_len * tile_len, HD)
    near_values = near[:, :, 1].reshape(chip_tiles, list_len * tile_len, HD)
    live_cells = jnp.repeat(near_live > 0, tile_len, axis=1)[:, None, :]

    scores = (
        jnp.einsum("sad,sbd->sab", query_h, near_keys, preferred_element_type=jnp.float32)
        * score_scale
    )
    row_peak = jnp.max(jnp.where(live_cells, scores, -1e30), axis=2, keepdims=True)
    row_total = jnp.sum(
        jnp.where(live_cells, jnp.exp(scores - row_peak), 0.0), axis=2, keepdims=True
    )
    log_total = row_peak + jnp.log(row_total)
    prob_full = jnp.where(live_cells, jnp.exp(scores - log_total), 0.0)
    prob_half = prob_full.astype(jnp.bfloat16)
    attn_h = jnp.einsum(
        "sab,sbd->sad", prob_half, near_values, preferred_element_type=jnp.float32
    ).astype(jnp.bfloat16)
    row_delta = jnp.einsum("sad,sad->sa", grad_h, attn_h, preferred_element_type=jnp.float32)
    grad_prob = jnp.einsum(
        "sad,sbd->sab", grad_h, near_values, preferred_element_type=jnp.float32
    )
    grad_score = (prob_full * (grad_prob - row_delta[:, :, None])).astype(jnp.bfloat16)
    grad_query_h = (
        jnp.einsum("sab,sbd->sad", grad_score, near_keys, preferred_element_type=jnp.float32)
        * score_scale
    ).astype(jnp.bfloat16)

    attn_tiles, grad_q = from_head((attn_h, grad_query_h), local_tiles, tile_len, heads_here)

    qg_all = lax.all_gather(
        jnp.stack([query_h, grad_h], axis=1), "z", axis=0, tiled=True
    )
    stats_all = lax.all_gather(
        jnp.stack([log_total[:, :, 0], row_delta], axis=1), "z", axis=0, tiled=True
    )

    owned_slots = first_slot + jnp.arange(chip_tiles, dtype=jnp.int32)
    pair_hits = (key_slot[:, :, None] == owned_slots[None, None, :]) & (live_mask[:, :, None] > 0)
    named_by = jnp.any(pair_hits, axis=1).astype(jnp.int32)
    rank_of = jnp.cumsum(named_by, axis=0) - 1
    list_pos = jnp.arange(list_len, dtype=jnp.int32)
    placed = (named_by[:, :, None] > 0) & (rank_of[:, :, None] == list_pos[None, None, :])
    slot_index = jnp.arange(tile_count, dtype=jnp.int32)
    picked = jnp.sum(placed.astype(jnp.int32) * slot_index[:, None, None], axis=0)
    picked_live = jnp.any(placed, axis=0)

    rows = qg_all[picked.reshape(-1)].reshape(chip_tiles, list_len, 2, tile_len, HD)
    query_rows = rows[:, :, 0].reshape(chip_tiles, list_len * tile_len, HD)
    grad_rows = rows[:, :, 1].reshape(chip_tiles, list_len * tile_len, HD)
    stat_rows = stats_all[picked.reshape(-1)].reshape(chip_tiles, list_len, 2, tile_len)
    total_rows = stat_rows[:, :, 0].reshape(chip_tiles, 1, list_len * tile_len)
    delta_rows = stat_rows[:, :, 1].reshape(chip_tiles, 1, list_len * tile_len)
    keep_pair = jnp.repeat(picked_live, tile_len, axis=1)[:, None, :]

    owner_scores = (
        jnp.einsum("tbd,tad->tba", key_h, query_rows, preferred_element_type=jnp.float32)
        * score_scale
    )
    owner_probs = jnp.where(keep_pair, jnp.exp(owner_scores - total_rows), 0.0)
    owner_grad_prob = jnp.einsum(
        "tbd,tad->tba", value_h, grad_rows, preferred_element_type=jnp.float32
    )
    owner_grad_score = (owner_probs * (owner_grad_prob - delta_rows)).astype(jnp.bfloat16)
    grad_key_h = (
        jnp.einsum("tba,tad->tbd", owner_grad_score, query_rows, preferred_element_type=jnp.float32)
        * score_scale
    ).astype(jnp.bfloat16)
    grad_value_h = jnp.einsum(
        "tba,tad->tbd", owner_probs.astype(jnp.bfloat16), grad_rows, preferred_element_type=jnp.float32
    ).astype(jnp.bfloat16)

    grad_k, grad_v = from_head((grad_key_h, grad_value_h), local_tiles, tile_len, heads_here)

    attn_flat = attn_tiles.reshape(local_tiles * tile_len, col_width)
    grad_weight = lax.psum_scatter(
        lax.dot_general(
            full_rows, attn_flat, (((0,), (0,)), ((), ())), preferred_element_type=jnp.float32
        ).astype(jnp.bfloat16),
        ("z", "core"),
        scatter_dimension=0,
        tiled=True,
    )
    return (grad_q, grad_k, grad_v, grad_weight)


def solution(mesh):
    ctx_count = mesh.shape["ctx"]
    tp_count = mesh.shape["tp"]
    devices = mesh.devices.reshape(ctx_count // CORES, CORES, tp_count)
    chip_mesh = Mesh(devices, ("z", "core", "tp"))
    tiles = ("z", "core")
    in_specs = (
        P(tiles, None, "tp"),
        P(tiles, None, "tp"),
        P(tiles, None, "tp"),
        P((*tiles, "tp"), None),
        P(None, "tp"),
        P(),
        P(),
        P(),
    )
    out_specs = (
        P(tiles, None, "tp"),
        P(tiles, None, "tp"),
        P(tiles, None, "tp"),
        P(tiles, "tp"),
    )
    return jax.shard_map(
        per_device, mesh=chip_mesh, in_specs=in_specs, out_specs=out_specs, check_vma=False
    )
```

time: 344 us -> 260 us (0.76)
  local copies, waits for them, and re-layouts: 126 us -> 40.9 us
  blocking collectives: 16.2 us -> 39 us
  waiting for transfers between devices: 144 us -> 129 us
  matrix products: 36.7 us -> 29.6 us
    gather x34 -> x3, local copies, waits for them, and re-layouts: 66.4 us -> 17.1 us  [the longest x1 8.18 us: per_device(): kv_all[near_slots.reshape(-1)]]
    reshape x10 -> x2, local copies, waits for them, and re-layouts: 42 us -> 0.16 us  [the longest x1 0.08 us: per_device(): near_slots.reshape(-1)]
    all_gather x3 -> x2, waiting for transfers between devices: 82.6 us -> 50.9 us  [the longest x1 50.9 us: per_device(): kv_all = lax.all_gather(head_parts[:, 1:3], 'z', axis=0, tiled=True)]
    all_to_all x0 -> x3, blocking collectives: none -> 18.3 us  [the longest x2 13.3 us: from_head(): lax.all_to_all(stacked, 'core', split_axis=0, concat_axis=3, tiled=True)]
    reduce_scatter x1, waiting for transfers between devices: 0.01 us -> 17.8 us  [per_device(): lax.psum_scatter(lax.dot_general(full_rows, attn_flat, (((0,), (0,)), (()...]
    slice x0 -> x9, local copies, waits for them, and re-layouts: none -> 10.6 us  [the longest x1 4.32 us: per_device(): query_rows = rows[:, :, 0].reshape(chip_tiles, list_len * tile_len, HD)]
    split x2 -> x0, local copies, waits for them, and re-layouts: 6.72 us -> none  [side_by_side(): jnp.split(out, [sum(widths[:k]) for k in range(1, len(widths))], axis=along)]
    dot_general x15 -> x6, matrix products: 27.3 us -> 20.9 us  [the longest x1 8.23 us: per_device(): jnp.einsum('tba,tad->tbd', owner_grad_score, query_rows, preferred_elemen...]
  transfers between devices with their start and end apart: 5 -> 4, of which waited for: 3 -> 3; matrix products, arithmetic and copies ran while one was open for 48% -> 25% of each run, Pallas kernels for 0% -> 0%
where the time goes in v1:
time: 260 us; the launch traced here: 257 us
  waiting for transfers between devices  129 us (50%)
  local copies, waits for them, and re-layouts  40.9 us (16%)
  blocking collectives  39 us (15%)
  matrix products  29.6 us (11%)
  between operations  14.2 us (5%)
  other arithmetic  4.82 us (2%)
    all_gather x1, waiting for transfers between devices, per_device(): full_rows = lax.all_gather(grad_out, 'tp', axis=0, tiled=True)  59.2 us
    all_gather x1, waiting for transfers between devices, per_device(): kv_all = lax.all_gather(head_parts[:, 1:3], 'z', axis=0, tiled=True)  50.9 us
    all_gather x1, blocking collectives, per_device(): lax.all_gather(jnp.stack([log_total[:, :, 0], row_delta], axis=1), 'z', a...  20.7 us
    reduce_scatter x1, waiting for transfers between devices, per_device(): lax.psum_scatter(lax.dot_general(full_rows, attn_flat, (((0,), (0,)), (()...  17.8 us
    all_to_all x2, blocking collectives, from_head(): lax.all_to_all(stacked, 'core', split_axis=0, concat_axis=3, tiled=True)  13.3 us
    unnamed x26, local copies, waits for them, and re-layouts  8.29 us
    dot_general x1, matrix products, per_device(): jnp.einsum('tba,tad->tbd', owner_grad_score, query_rows, preferred_elemen...  8.23 us
    gather x1, local copies, waits for them, and re-layouts, per_device(): kv_all[near_slots.reshape(-1)]  8.18 us
  transfers between devices with their start and end apart: 4, of which 3 were waited for; matrix products, arithmetic and copies ran while one was open for 25% of the time, Pallas kernels for 0%

profile of v1, /device:TPU:1, one launch (start us, length us, event | category | flops | bytes accessed | tf_op | source)
XLA Modules:
  0.0 257.3 jit_solution(14067331215117245325)
XLA Ops:
  8.0 1.1 copy.56
  9.1 1.1 copy.55
  10.2 1.1 copy.54
  11.3 59.2 %all-gather.4.cloned.1.call-done = bf16[512,4096]{1,0:T(8,128)(2,1)} async-done(((bf16[32,4096]{1,0:T(8,128)(2,1)}), bf16[512,4096]{1,0:T(8,128)(2,1)}) %all-gather.4.cloned.1.call-update) | async-done | bytes 4194320 | tf_op jit(solution)/shard_map/all_gather | solution.py:52
  70.5 3.4 %convolution_convert_fusion.1 = bf16[512,256]{1,0:T(8,128)(2,1)S(1)} fusion(bf16[512,4096]{1,0:T(8,128)(2,1)} %all-gather.4.cloned.1.call-done, bf16[4096,256]{1,0:T(8,128)(2,1)S(1)} %copy-done), kind=kOutput, calls=%fused_computation.30 | convolution fusion | flops 1073872896 | bytes 6553600 | tf_op jit(solution)/shard_map/dot_general | solution.py:53
  75.0 5.0 %all_to_all.51 = bf16[4,4,128,2,128]{4,2,0,1,3:T(8,128)(2,1)S(1)} all-to-all(bf16[4,4,128,2,128]{4,2,0,1,3:T(8,128)(2,1)S(1)} %copy.58), channel_id=1, replica_groups=mesh['z'=8,'core'=2,'tp'=16] {'core'}, dimensions={3} | all-to-all | bytes 2097152 | tf_op jit(solution)/shard_map/all_to_all | solution.py:28
  80.2 0.8 slice.67
  81.1 0.8 pad_maximum_fusion.1
  84.3 50.9 %all-gather.6.cloned.1.call-done = bf16[64,2,128,128]{3,2,0,1:T(8,128)(2,1)} async-done(((bf16[8,2,128,128]{3,2,0,1:T(8,128)(2,1)}), bf16[64,2,128,128]{3,2,0,1:T(8,128)(2,1)}) %all-gather.6.cloned.1.call-update) | async-done | bytes 4194320 | tf_op jit(solution)/shard_map/all_gather | solution.py:62
  135.2 8.2 %gather_fusion = bf16[96,2,128,128]{3,2,1,0:T(8,128)(2,1)} fusion(bf16[64,2,128,128]{3,2,0,1:T(8,128)(2,1)} %all-gather.6.cloned.1.call-done, s32[1024]{0:T(1024)S(1)} %pad_clamp_fusion.1), kind=kCustom, calls=%fused_computation | custom fusion | bytes 12583296 | tf_op jit(solution)/shard_map/gather | solution.py:63
  143.4 4.2 %fusion.60 = (bf16[8,12,1,128,128]{4,3,2,1,0:T(8,128)(2,1)S(1)}, bf16[8,12,1,128,128]{4,3,2,1,0:T(8,128)(2,1)S(1)}) fusion(bf16[8,12,2,128,128]{4,3,2,1,0:T(8,128)(2,1)} %bitcast.99), kind=kLoop, calls=%fused_computation.93 | loop fusion | bytes 12582912 | tf_op jit(solution)/shard_map/slice | solution.py:65
  147.6 1.1 select_reduce_fusion.1
  148.8 1.5 select_reduce_fusion
  150.3 1.7 fusion.32
  152.1 7.5 %fusion.28 = bf16[8,1,128,128]{3,2,0,1:T(8,128)(2,1)S(1)} fusion(bf16[8,1536,128]{2,1,0:T(8,128)(2,1)} %bitcast.101, f32[8,128,1536]{2,1,0:T(8,128)} %copy-done.2, bf16[8,1536,128]{2,1,0:T(8,128)(2,1)} %bitcast.113, f32[8,128]{1,0:T(8,128)S(1)} %get-tuple-element.42, f32[8,128]{1,0:T(8,128)S(1)} %log_add_fusion, ...), kind=kOutput, calls=%fused_computation.33 | convolution fusion | flops 815005696 | bytes 13127680 | tf_op jit(solution)/shard_map/sab,sbd->sad/dot_general | solution.py:88
  159.8 4.7 %all_to_all.52 = bf16[8,2,128,1,128]{4,2,1,3,0:T(8,128)(2,1)S(1)} all-to-all(bf16[8,2,128,1,128]{4,2,1,3,0:T(8,128)(2,1)S(1)} %copy.62), channel_id=1, replica_groups=mesh['z'=8,'core'=2,'tp'=16] {'core'}, dimensions={0} | all-to-all | bytes 1048576 | tf_op jit(solution)/shard_map/all_to_all | solution.py:34
  165.4 4.8 %fusion = bf16[4096,256]{0,1:T(8,128)(2,1)} fusion(bf16[512,4096]{1,0:T(8,128)(2,1)} %all-gather.4.cloned.1.call-done, bf16[64,8,2,128]{3,2,1,0:T(2,128)(2,1)S(1)} %bitcast.119), kind=kOutput, calls=%fused_computation.10 | convolution fusion | flops 1074790400 | bytes 6553600 | tf_op jit(solution)/shard_map/dot_general | solution.py:140
  170.7 0.9 reshape_squeeze.25
  171.5 20.7 %all_gather.15 = f32[64,2,128]{2,1,0:T(2,128)S(1)} all-gather(f32[8,2,128]{2,1,0:T(2,128)S(1)} %pad_maximum_fusion.2), channel_id=1, replica_groups=mesh['z'=8,'core'=2,'tp'=16] {'z'}, dimensions={0}, use_global_device_ids=true | all-gather | bytes 73728 | tf_op jit(solution)/shard_map/all_gather | solution.py:97
  192.2 0.7 gather_fusion.2
  193.0 8.2 %gather_fusion.1 = bf16[96,2,128,128]{3,2,1,0:T(8,128)(2,1)} fusion(bf16[64,2,128,128]{3,2,0,1:T(8,128)(2,1)} %all-gather.8.cloned.1.call-done, s32[1024]{0:T(1024)S(1)} %pad_clamp_fusion), kind=kCustom, calls=%fused_computation.1 | custom fusion | bytes 12583296 | tf_op jit(solution)/shard_map/gather | solution.py:111
  201.4 4.3 %fusion.59 = (bf16[8,12,1,128,128]{4,3,2,1,0:T(8,128)(2,1)S(1)}, bf16[8,12,1,128,128]{4,3,2,1,0:T(8,128)(2,1)S(1)}) fusion(bf16[8,12,2,128,128]{4,3,2,1,0:T(8,128)(2,1)} %bitcast.98), kind=kLoop, calls=%fused_computation.92 | loop fusion | bytes 12582912 | tf_op jit(solution)/shard_map/slice | solution.py:112
  205.8 1.0 fusion.35
  206.8 3.0 %copy-done.5 = f32[8,128,1536]{2,1,0:T(8,128)} copy-done((f32[8,128,1536]{2,1,0:T(8,128)}, f32[8,128,1536]{2,1,0:T(8,128)S(1)}, u32[]{:S(2)}) %copy-start.5) | copy-done | bytes 6291480
  209.8 1.4 fusion.29
  211.2 8.2 %fusion.27 = bf16[8,1,128,128]{3,2,0,1:T(8,128)(2,1)} fusion(bf16[8,1536,128]{2,1,0:T(8,128)(2,1)} %bitcast.103, f32[8,128,1536]{2,1,0:T(8,128)} %copy-done.5, bf16[8,1536,128]{2,1,0:T(8,128)(2,1)} %bitcast.115, f32[8,1536]{1,0:T(8,128)S(1)} %get-tuple-element.44, f32[8,1536]{1,0:T(8,128)S(1)} %get-tuple-element.45, ...), kind=kOutput, calls=%fused_computation.32 | convolution fusion | flops 815005696 | bytes 13217792 | tf_op jit(solution)/shard_map/tba,tad->tbd/dot_general | solution.py:129
  219.4 1.0 maximum_bitcast_fusion.1
  220.5 8.5 %all_to_all.53 = bf16[8,2,128,1,128]{4,2,1,3,0:T(8,128)(2,1)S(1)} all-to-all(bf16[8,2,128,1,128]{4,2,1,3,0:T(8,128)(2,1)S(1)} %copy.67), channel_id=1, replica_groups=mesh['z'=8,'core'=2,'tp'=16] {'core'}, dimensions={0} | all-to-all | bytes 1048576 | tf_op jit(solution)/shard_map/all_to_all | solution.py:34
  229.4 0.9 reshape_squeeze.28
  230.5 0.9 reshape_squeeze.29
  231.4 17.8 %reduce-scatter.2.cloned.1.call-done = bf16[256,256]{0,1:T(8,128)(2,1)} async-done(((bf16[4096,256]{0,1:T(8,128)(2,1)}), bf16[256,256]{0,1:T(8,128)(2,1)}) %reduce-scatter.2.cloned.1.call-update) | async-done | bytes 131088 | tf_op jit(solution)/shard_map/reduce_scatter | solution.py:139
  249.1 1.7 copy.70
  (72 shorter events, 6.8 us)
Async XLA Ops:
  7.2 63.3 %copy-start = (bf16[4096,256]{1,0:T(8,128)(2,1)S(1)}, bf16[4096,256]{1,0:T(8,128)(2,1)}, u32[]{:S(2)}) copy-start(bf16[4096,256]{1,0:T(8,128)(2,1)} %param.12) | copy-start | bytes 6291460
  7.2 63.3 %all-gather.4.cloned.1.call-start = ((), (), s32[]{:S(2)}) async-start(), calls=%async_computation.4 | async-start | bytes 4456448 | tf_op jit(solution)/shard_map/all_gather | solution.py:52
  7.9 127.3 %all-gather.6.cloned.1.call-start = ((), (), s32[]{:S(2)}) async-start(), calls=%async_computation.5 | async-start | bytes 4718592 | tf_op jit(solution)/shard_map/all_gather | solution.py:62
  74.2 8.0 %copy-start.8 = (s32[64]{0:T(128)S(1)}, s32[64]{0:T(128)}, u32[]{:S(2)}) copy-start(s32[64]{0:T(128)} %param.15) | copy-start | bytes 772
  74.2 8.0 %copy-start.9 = (s32[64,12]{0,1:T(8,128)S(1)}, s32[64,12]{0,1:T(8,128)}, u32[]{:S(2)}) copy-start(s32[64,12]{0,1:T(8,128)} %param.13) | copy-start | bytes 9220
  74.2 8.9 %copy-start.10 = (s32[64,12]{0,1:T(8,128)S(1)}, s32[64,12]{0,1:T(8,128)}, u32[]{:S(2)}) copy-start(s32[64,12]{0,1:T(8,128)} %param.14) | copy-start | bytes 9220
  81.0 111.9 %all-gather.8.cloned.1.call-start = ((), (), s32[]{:S(2)}) async-start(), calls=%async_computation.6 | async-start | bytes 4718592 | tf_op jit(solution)/shard_map/all_gather | solution.py:94
  82.0 167.2 %reduce-scatter.2.cloned.1.call-start = ((), (), s32[]{:S(2)}) async-start(), calls=%async_computation.7 | async-start | bytes 2228224 | tf_op jit(solution)/shard_map/reduce_scatter | solution.py:139
  147.6 2.7 %copy-start.3 = (bf16[8,12,1,128,128]{4,3,2,1,0:T(8,128)(2,1)}, bf16[8,12,1,128,128]{4,3,2,1,0:T(8,128)(2,1)S(1)}, u32[]{:S(2)}) copy-start(bf16[8,12,1,128,128]{4,3,2,1,0:T(8,128)(2,1)S(1)} %get-tuple-element.29) | copy-start | bytes 9437188
  147.6 2.7 %copy-start.6 = (bf16[8,12,1,128,128]{4,3,2,1,0:T(8,128)(2,1)}, bf16[8,12,1,128,128]{4,3,2,1,0:T(8,128)(2,1)S(1)}, u32[]{:S(2)}) copy-start(bf16[8,12,1,128,128]{4,3,2,1,0:T(8,128)(2,1)S(1)} %get-tuple-element.28) | copy-start | bytes 9437188
  148.8 3.4 %copy-start.2 = (f32[8,128,1536]{2,1,0:T(8,128)}, f32[8,128,1536]{2,1,0:T(8,128)S(1)}, u32[]{:S(2)}) copy-start(f32[8,128,1536]{2,1,0:T(8,128)S(1)} %get-tuple-element.41) | copy-start | bytes 18874372
  205.8 5.4 %copy-start.4 = (bf16[8,12,1,128,128]{4,3,2,1,0:T(8,128)(2,1)}, bf16[8,12,1,128,128]{4,3,2,1,0:T(8,128)(2,1)S(1)}, u32[]{:S(2)}) copy-start(bf16[8,12,1,128,128]{4,3,2,1,0:T(8,128)(2,1)S(1)} %get-tuple-element.26) | copy-start | bytes 9437188
  205.8 5.4 %copy-start.7 = (bf16[8,12,1,128,128]{4,3,2,1,0:T(8,128)(2,1)}, bf16[8,12,1,128,128]{4,3,2,1,0:T(8,128)(2,1)S(1)}, u32[]{:S(2)}) copy-start(bf16[8,12,1,128,128]{4,3,2,1,0:T(8,128)(2,1)S(1)} %get-tuple-element.27) | copy-start | bytes 9437188
  206.8 3.1 %copy-start.5 = (f32[8,128,1536]{2,1,0:T(8,128)}, f32[8,128,1536]{2,1,0:T(8,128)S(1)}, u32[]{:S(2)}) copy-start(f32[8,128,1536]{2,1,0:T(8,128)S(1)} %fusion.35) | copy-start | bytes 18874372
  211.2 39.6 %copy-start.1 = (bf16[4096,256]{1,0:T(8,128)(2,1)S(1)}, bf16[4096,256]{1,0:T(8,128)(2,1)}, u32[]{:S(2)}) copy-start(bf16[4096,256]{1,0:T(8,128)(2,1)} %param.12) | copy-start | bytes 6291460
Sparse Core Ops, SparseCore 0:
  10.4 60.0 all-gather.3
  81.1 54.0 all-gather.5
  137.0 53.8 all-gather.7
  193.3 55.8 reduce-scatter.1
